TPU v7x, 256 devices: a whole 4x4x8 slice. The times are simulated.
256 devices in a mesh: dp: 4 (over y), seq: 64 (over z, x, core).
Axes of the slice: x: 4, y: 4, z: 8, core: 2. Of those that a mesh axis runs over, the one named last changes fastest.
Arguments:
- features: bfloat16 [49152, 1408], P(('dp', 'seq')), parts along dimension 0, may hold values from -6 to 6
- norm_gain: float32 [1408], replicated, may hold values from 0.1 to 1.9
- conv_weight: bfloat16 [5, 1408, 1536], P(None, None, 'seq'), may hold values from -0.0625 to 0.0625
- conv_bias: float32 [1536], replicated, may hold values from -3 to 3
- attn_gain: float32 [1536], replicated, may hold values from 0.1 to 1.9
- query_weight: bfloat16 [1536, 1024], P('seq'), may hold values from -1 to 1
- keyval_weight: bfloat16 [1536, 256], P('seq'), may hold values from -1 to 1
- head_scale: float32 [8], replicated, may hold values from 1 to 4
- output_weight: bfloat16 [1024, 1536], P('seq'), may hold values from -0.1875 to 0.1875
Outputs:
- coarse: bfloat16 [24576, 1536], P(('dp', 'seq')), parts along dimension 0
- attended: bfloat16 [24576, 1536], P(('dp', 'seq')), parts along dimension 0
There are 4 independent parts, one for each index of `dp`. A program takes and returns all parts, laid end to end along the dimension named above; an argument that names none is the same for every part. Nothing has to cross between parts.
All inputs are finite; a program needn't handle non-finite values.
Results may differ from a plain program's by a relative error of at most 0.007.
Values may be sent and summed in bfloat16 or wider, within the bound.
No kernel may reach another device: no remote copies, remote signals or barrier semaphores. Data moves between devices by JAX's collectives and lax.ppermute only.
A program may use at most 128 MiB of HBM per device.

v0:
```python
import jax
import jax.numpy as jnp
from jax import lax
from jax.sharding import Mesh
from jax.sharding import PartitionSpec as P

HEAD_DIM = 128


def normalize(values_in, channel_gain):
    meansq = jnp.mean(values_in * values_in, axis=-1, keepdims=True)
    return values_in * lax.rsqrt(meansq + 1e-06) * channel_gain


def convolve(padded, kernel, row_count):
    summed = jnp.zeros((row_count, kernel.shape[2]), jnp.float32)
    for kernel_tap in range(kernel.shape[0]):
        summed = summed + jnp.dot(
            padded[kernel_tap : kernel_tap + row_count],
            kernel[kernel_tap],
            preferred_element_type=jnp.float32,
        )
    return summed


def pool_pairs(levels):
    return jnp.max(levels.reshape(-1, 2, levels.shape[1]), axis=1)


def spread_in_plane(block):
    inner = lax.all_gather(block, "sxx", axis=0, tiled=True)
    return lax.all_gather(inner, "core", axis=0, tiled=True)


def plane_order(columns, nz, nxx, nc):
    rows = columns.shape[0]
    return (
        columns.reshape(rows, nz, nxx, nc, -1)
        .transpose(0, 3, 2, 1, 4)
        .reshape(rows, columns.shape[1])
    )


def attend(queries, key_block, scales):
    row_count = queries.shape[0]
    head_count = scales.shape[0]
    shaped = queries.reshape(row_count, head_count, HEAD_DIM)
    key_part = key_block[:, :HEAD_DIM]
    value_part = key_block[:, HEAD_DIM:]
    scores = (
        jnp.einsum("qhd,kd->hqk", shaped, key_part, preferred_element_type=jnp.float32)
        * scales[:, None, None]
        * HEAD_DIM ** (-0.5)
    )
    biggest = jnp.max(scores, axis=2)
    expon = jnp.exp(scores - biggest[:, :, None])
    total = jnp.sum(expon, axis=2)
    context = jnp.einsum(
        "hqk,kd->hqd", expon.astype(jnp.bfloat16), value_part, preferred_element_type=jnp.float32
    )
    context = context / total[:, :, None]
    return context.transpose(1, 0, 2).reshape(row_count, head_count * HEAD_DIM).astype(jnp.bfloat16)


def shards(
    features,
    norm_gain,
    conv_weight,
    conv_bias,
    attn_gain,
    query_weight,
    keyval_weight,
    head_scale,
    output_weight,
):
    nz = lax.axis_size("sz")
    nxx = lax.axis_size("sxx")
    nc = lax.axis_size("core")
    nx = nxx * nc
    me_x = lax.axis_index("sxx") * nc + lax.axis_index("core")
    rows_here = features.shape[0]
    taps, ch_in, width = conv_weight.shape
    ch_out = conv_bias.shape[0]
    proj_piece = jnp.concatenate([query_weight, keyval_weight], axis=1)
    pieces = [conv_weight, proj_piece, output_weight]
    sizes = [p.size for p in pieces]
    flat = jnp.concatenate([p.reshape(-1) for p in pieces])
    got = lax.all_gather(flat, "sz", axis=0, tiled=False)
    kernel = (
        got[:, : sizes[0]]
        .reshape(nz, taps, ch_in, width)
        .transpose(1, 2, 0, 3)
        .reshape(taps, ch_in, nz * width)
    )
    proj_z = got[:, sizes[0] : sizes[0] + sizes[1]].reshape(
        nz * proj_piece.shape[0], proj_piece.shape[1]
    )
    out_z = got[:, sizes[0] + sizes[1] :].reshape(
        nz * output_weight.shape[0], output_weight.shape[1]
    )
    normed = jax.nn.gelu(normalize(features.astype(jnp.float32), norm_gain)).astype(jnp.bfloat16)
    plane = lax.all_gather(normed, ("sxx", "core"), axis=0, tiled=True)
    plane_rows = plane.shape[0]
    forward = [(i, i + 1) for i in range(nz - 1)]
    backward = [(i + 1, i) for i in range(nz - 1)]
    low = lax.ppermute(plane[plane_rows - 2 :], "sz", forward)
    high = lax.ppermute(plane[:2], "sz", backward)
    padded = jnp.concatenate([low, plane, high], axis=0)
    bias_all = conv_bias.reshape(nz, nx, width).transpose(1, 0, 2)
    bias = lax.dynamic_index_in_dim(bias_all, me_x, axis=0, keepdims=False).reshape(nz * width)
    levels = convolve(padded, kernel, plane_rows) + bias[None, :]
    pooled = pool_pairs(levels).astype(jnp.bfloat16)
    proj_weight = spread_in_plane(proj_z)
    coarse_rows = rows_here // 2
    parts = pooled.reshape(nx, coarse_rows, nz * width)
    received = lax.all_to_all(parts, ("sxx", "core"), 0, 0, tiled=False)
    coarse = (
        received.reshape(nx, coarse_rows, nz, width)
        .transpose(1, 2, 0, 3)
        .reshape(coarse_rows, ch_out)
    )
    attn_in = normalize(coarse.astype(jnp.float32), attn_gain).astype(jnp.bfloat16)
    proj = jnp.dot(
        plane_order(attn_in, nz, nxx, nc), proj_weight, preferred_element_type=jnp.float32
    )
    q_cols = query_weight.shape[1]
    queries = proj[:, :q_cols].astype(jnp.bfloat16)
    keyvals = proj[:, q_cols:].astype(jnp.bfloat16)
    key_block = spread_in_plane(lax.all_gather(keyvals, "sz", axis=0, tiled=True))
    out_weight = spread_in_plane(out_z)
    context = attend(queries, key_block, head_scale)
    projected = jnp.dot(
        plane_order(context, nz, nxx, nc), out_weight, preferred_element_type=jnp.float32
    )
    return (coarse, projected.astype(jnp.bfloat16))


def solution(mesh):
    dp = mesh.shape["dp"]
    seq = mesh.shape["seq"]
    nc = 2 if seq % 2 == 0 else 1
    nxx = 4 if seq // nc % 4 == 0 else seq // nc
    nz = seq // (nc * nxx)
    grid = Mesh(mesh.devices.reshape(dp, nz, nxx, nc), ("dp", "sz", "sxx", "core"))
    seq_axes = ("sz", "sxx", "core")
    rows = P(("dp",) + seq_axes, None)
    return jax.shard_map(
        shards,
        mesh=grid,
        in_specs=(
            rows,
            P(),
            P(None, None, seq_axes),
            P(),
            P(),
            P(seq_axes, None),
            P(seq_axes, None),
            P(),
            P(seq_axes, None),
        ),
        out_specs=(rows, rows),
        check_vma=False,
    )
```

profile of v0, /device:TPU:1, one launch (start us, length us, event | category | flops | bytes accessed | tf_op | source)
XLA Modules:
  0.0 313.2 jit_solution(10841448251101722798)
XLA Ops:
  7.3 2.1 copy.56
  9.4 2.4 reshape.100
  12.1 0.8 pad_maximum_fusion.2
  13.1 1.3 fusion.37
  14.5 51.2 %all-gather.24.cloned.1.call-done = bf16[1794048]{0:T(1024)(128)(2,1)} async-done(((bf16[224256]{0:T(1024)(128)(2,1)}), bf16[1794048]{0:T(1024)(128)(2,1)}) %all-gather.24.cloned.1.call-update) | async-done | bytes 3588112 | tf_op jit(solution)/shard_map/all_gather | solution.py:88
  65.7 5.4 %reshape.114 = bf16[8,224256]{1,0:T(8,128)(2,1)} reshape(bf16[1794048]{0:T(1024)(128)(2,1)} %all-gather.24.cloned.1.call-done) | data formatting | bytes 7176192 | tf_op jit(solution)/shard_map/all_gather | solution.py:88
  71.1 1.2 slice.95
  72.3 1.1 reshape.109
  73.6 2.8 reshape.124
  76.4 22.4 %reshape.103 = bf16[8,5,1408,24]{3,2,1,0:T(8,128)(2,1)} reshape(bf16[1351680]{0:T(1024)(128)(2,1)} %reshape.124) | data formatting | bytes 5406720 | tf_op jit(solution)/shard_map/reshape | solution.py:91
  98.8 10.0 %fusion.56 = (bf16[1,1408,8,24]{3,1,0,2:T(8,128)(2,1)S(1)}, bf16[1,1408,8,24]{3,1,0,2:T(8,128)(2,1)}, bf16[1,1408,8,24]{3,1,0,2:T(8,128)(2,1)}, bf16[1,1408,8,24]{3,1,0,2:T(8,128)(2,1)}, bf16[1,1408,8,24]{3,1,0,2:T(8,128)(2,1)}) fusion(bf16[5,1408,8,24]{3,1,0,2:T(8,128)(2,1)} %bitcast.78), kind=kLoop, calls=%fused_computation.61 | loop fusion | bytes 5406720 | tf_op jit(solution)/shard_map/slice | solution.py:20
  108.8 3.7 %copy.58 = bf16[1,1408,8,24]{1,3,2,0:T(8,128)(2,1)} copy(bf16[1,1408,8,24]{3,1,0,2:T(8,128)(2,1)} %get-tuple-element.13) | data formatting | bytes 1081344 | tf_op jit(solution)/shard_map/slice | solution.py:20
  112.5 3.8 %copy.59 = bf16[1,1408,8,24]{1,3,2,0:T(8,128)(2,1)} copy(bf16[1,1408,8,24]{3,1,0,2:T(8,128)(2,1)} %get-tuple-element.12) | data formatting | bytes 1081344 | tf_op jit(solution)/shard_map/slice | solution.py:20
  116.4 3.8 %copy.57 = bf16[1,1408,8,24]{1,3,2,0:T(8,128)(2,1)} copy(bf16[1,1408,8,24]{3,1,0,2:T(8,128)(2,1)} %get-tuple-element.14) | data formatting | bytes 1081344 | tf_op jit(solution)/shard_map/slice | solution.py:20
  120.2 3.8 %copy.61 = bf16[1,1408,8,24]{1,3,2,0:T(8,128)(2,1)} copy(bf16[1,1408,8,24]{3,1,0,2:T(8,128)(2,1)} %get-tuple-element.11) | data formatting | bytes 1081344 | tf_op jit(solution)/shard_map/slice | solution.py:20
  124.0 1.7 copy.60
  125.7 0.8 fusion.57
  126.5 1.3 collective-permute-start
  127.8 1.5 collective-permute-start.1
  129.3 6.1 %all-gather.12.cloned.1.call-done = bf16[768,1280]{1,0:T(8,128)(2,1)} async-done(((bf16[192,1280]{1,0:T(8,128)(2,1)}), bf16[768,1280]{1,0:T(8,128)(2,1)}) %all-gather.12.cloned.1.call-update) | async-done | bytes 1966096 | tf_op jit(solution)/shard_map/all_gather | solution.py:31
  135.4 2.7 constant_dynamic-update-slice_fusion.1
  138.2 0.8 slice-done.3
  139.1 1.6 fusion.58
  140.7 1.6 fusion.12
  142.3 1.6 fusion.8
  143.9 1.6 fusion.26
  145.6 1.7 fusion.20
  147.3 0.3 copy.62
  147.6 0.4 reshape.105
  147.9 2.2 reduce_max.18
  150.3 0.4 convert_element_type.45
  150.8 0.8 copy.64
  151.6 4.2 %all-to-all-start = ((bf16[8,96,192]{1,2,0:T(8,128)(2,1)}), bf16[8,96,192]{1,2,0:T(8,128)(2,1)S(1)}, u32[]{:S(2)}, u32[]{:S(2)}) async-start(bf16[8,96,192]{1,2,0:T(8,128)(2,1)} %copy.64), calls=%async_computation | async-start | bytes 786432 | tf_op jit(solution)/shard_map/all_to_all | solution.py:116
  155.9 7.6 %all-to-all-done = bf16[8,96,192]{1,2,0:T(8,128)(2,1)S(1)} async-done(((bf16[8,96,192]{1,2,0:T(8,128)(2,1)}), bf16[8,96,192]{1,2,0:T(8,128)(2,1)S(1)}, u32[]{:S(2)}, u32[]{:S(2)}) %all-to-all-start) | async-done | bytes 294944 | tf_op jit(solution)/shard_map/all_to_all | solution.py:116
  163.5 0.2 multiply_reduce_fusion
  163.7 0.3 fusion.50
  164.1 2.8 convolution_convert_fusion.1
  166.9 22.5 %all_gather.35 = bf16[768,256]{1,0:T(8,128)(2,1)} all-gather(bf16[96,256]{1,0:T(8,128)(2,1)S(1)} %slice.96), channel_id=1, replica_groups=mesh['dp'=4,'sz'=8,'sxx'=4,'core'=2] {'sz'}, dimensions={0}, use_global_device_ids=true | all-gather | bytes 442368 | tf_op jit(solution)/shard_map/all_gather | solution.py:129
  189.5 0.9 reshape.112
  190.5 32.7 %all-gather.16.cloned.1.call-done = bf16[3072,256]{1,0:T(8,128)(2,1)} async-done(((bf16[768,256]{1,0:T(8,128)(2,1)}), bf16[3072,256]{1,0:T(8,128)(2,1)}) %all-gather.16.cloned.1.call-update) | async-done | bytes 1572880 | tf_op jit(solution)/shard_map/all_gather | solution.py:31
  223.2 0.3 all-gather.22.cloned.1.call-start
  223.5 0.9 copy.71
  224.4 29.5 %all-gather.20.cloned.1.call-done = bf16[512,1536]{1,0:T(8,128)(2,1)} async-done(((bf16[128,1536]{1,0:T(8,128)(2,1)}), bf16[512,1536]{1,0:T(8,128)(2,1)}) %all-gather.20.cloned.1.call-update) | async-done | bytes 1572880 | tf_op jit(solution)/shard_map/all_gather | solution.py:31
  253.9 20.2 %all-gather.18.cloned.1.call-done = bf16[6144,256]{1,0:T(8,128)(2,1)} async-done(((bf16[3072,256]{1,0:T(8,128)(2,1)}), bf16[6144,256]{1,0:T(8,128)(2,1)}) %all-gather.18.cloned.1.call-update) | async-done | bytes 3145744 | tf_op jit(solution)/shard_map/all_gather | solution.py:32
  274.1 9.2 %bitcast_reduce_fusion = (f32[8,96]{1,0:T(8,128)S(1)}, f32[6144,96,8]{0,1,2:T(8,128)}) fusion(f32[8]{0:T(128)S(1)} %copy-done.8, bf16[6144,256]{1,0:T(8,128)(2,1)} %all-gather.18.cloned.1.call-done, bf16[96,1280]{1,0:T(8,128)(2,1)S(1)} %convolution_convert_fusion.1), kind=kOutput, calls=%fused_computation.1 | convolution fusion | flops 1222114560 | bytes 20647424 | tf_op jit(solution)/shard_map/qhd,kd->hqk/dot_general | solution.py:51
  283.3 11.1 %fusion.1 = f32[8,96]{1,0:T(8,128)S(1)} fusion(f32[6144,96,8]{0,1,2:T(8,128)} %get-tuple-element.18, f32[8,96]{1,0:T(8,128)S(1)} %get-tuple-element.17, f32[8]{0:T(128)S(1)} %copy-done.8), kind=kLoop, calls=%fused_computation.4 | loop fusion | flops 18873600 | bytes 18880544 | tf_op jit(solution)/shard_map/reduce_sum | solution.py:57
  294.4 8.4 %fusion.46 = bf16[96,8,128]{2,0,1:T(8,128)(2,1)S(1)} fusion(bf16[6144,256]{1,0:T(8,128)(2,1)S(1)} %copy-done.1, f32[6144,96,8]{0,1,2:T(8,128)} %get-tuple-element.18, f32[8,96]{1,0:T(8,128)S(1)} %get-tuple-element.17, f32[8]{0:T(128)S(1)} %copy-done.8, f32[96,8]{0,1:T(8,128)S(1)} %bitcast.93), kind=kOutput, calls=%fused_computation.43 | convolution fusion | flops 1227030528 | bytes 20652544 | tf_op jit(solution)/shard_map/hqk,kd->hqd/dot_general | solution.py:58
  303.1 3.3 %convolution_convert_fusion = bf16[96,1536]{1,0:T(8,128)(2,1)} fusion(bf16[96,1024]{0,1:T(8,128)(2,1)S(1)} %bitcast.86, bf16[1024,1536]{1,0:T(8,128)(2,1)} %all-gather.22.cloned.1.call-done), kind=kOutput, calls=%fused_computation.23 | convolution fusion | flops 302137344 | bytes 3637248 | tf_op jit(solution)/shard_map/dot_general | solution.py:132
  (71 shorter events, 1.7 us)
Async XLA Ops:
  7.2 4.6 %copy-start.7 = (bf16[24,1024]{1,0:T(8,128)(2,1)S(1)}, bf16[24,1024]{1,0:T(8,128)(2,1)}, u32[]{:S(2)}) copy-start(bf16[24,1024]{1,0:T(8,128)(2,1)} %param.14) | copy-start | bytes 147460
  7.2 4.6 %copy-start.9 = (bf16[24,256]{1,0:T(8,128)(2,1)S(1)}, bf16[24,256]{1,0:T(8,128)(2,1)}, u32[]{:S(2)}) copy-start(bf16[24,256]{1,0:T(8,128)(2,1)} %param.15) | copy-start | bytes 36868
  7.2 4.8 %copy-start.6 = (bf16[16,1536]{1,0:T(8,128)(2,1)S(1)}, bf16[16,1536]{1,0:T(8,128)(2,1)}, u32[]{:S(2)}) copy-start(bf16[16,1536]{1,0:T(8,128)(2,1)} %param.17) | copy-start | bytes 147460
  7.2 5.7 %copy-start = (bf16[192,1408]{1,0:T(8,128)(2,1)S(1)}, bf16[192,1408]{1,0:T(8,128)(2,1)}, u32[]{:S(2)}) copy-start(bf16[192,1408]{1,0:T(8,128)(2,1)} %param.9) | copy-start | bytes 1622020
  7.2 5.9 %copy-start.10 = (f32[1408]{0:T(1024)S(1)}, f32[1408]{0:T(1024)}, u32[]{:S(2)}) copy-start(f32[1408]{0:T(1024)} %param.10) | copy-start | bytes 16900
  7.2 58.5 %all-gather.24.cloned.1.call-start = ((), (), s32[]{:S(2)}) async-start(), calls=%async_computation.8 | async-start | bytes 4036608 | tf_op jit(solution)/shard_map/all_gather | solution.py:88
  12.9 112.8 %all-gather.10.cloned.1.call-start = ((), (), s32[]{:S(2)}) async-start(), calls=%async_computation.1 | async-start | bytes 4866048 | tf_op jit(solution)/shard_map/all_gather | solution.py:102
  14.5 59.0 %copy-start.11 = (f32[1536]{0:T(1024)S(1)}, f32[1536]{0:T(1024)}, u32[]{:S(2)}) copy-start(f32[1536]{0:T(1024)} %param.12) | copy-start | bytes 18436
  14.5 120.9 %all-gather.12.cloned.1.call-start = ((), (), s32[]{:S(2)}) async-start(), calls=%async_computation.2 | async-start | bytes 2457600 | tf_op jit(solution)/shard_map/all_gather | solution.py:31
  71.1 2.6 slice-start
  73.4 90.7 %all-gather.14.cloned.1.call-start = ((), (), s32[]{:S(2)}) async-start(), calls=%async_computation.3 | async-start | bytes 5898240 | tf_op jit(solution)/shard_map/all_gather | solution.py:32
  126.5 14.2 %collective-permute-start = (bf16[2,1408]{1,0:T(2,128)(2,1)S(1)}, bf16[2,1408]{1,0:T(2,128)(2,1)S(1)}, u32[]{:S(2)}, u32[]{:S(2)}) collective-permute-start(bf16[2,1408]{1,0:T(2,128)(2,1)S(1)} %get-tuple-element.15), channel_id=1, source_target_pairs={{0,8},{8,16},{16,24},{24,32},{32,40},{40,48},{48,56},{1,9},{9,17},... | collective-permute-start | bytes 16904 | tf_op jit(solution)/shard_map/ppermute | solution.py:106
  127.8 12.8 %collective-permute-start.1 = (bf16[2,1408]{1,0:T(2,128)(2,1)S(1)}, bf16[2,1408]{1,0:T(2,128)(2,1)S(1)}, u32[]{:S(2)}, u32[]{:S(2)}) collective-permute-start(bf16[2,1408]{1,0:T(2,128)(2,1)S(1)} %get-tuple-element.16), channel_id=1, source_target_pairs={{8,0},{16,8},{24,16},{32,24},{40,32},{48,40},{56,48},{9,1},{17,9},... | collective-permute-start | bytes 16904 | tf_op jit(solution)/shard_map/ppermute | solution.py:107
  135.4 2.8 slice-start.2
  135.4 3.5 %slice-start.3 = ((s8[4325376]{0:T(1024)(128)(4,1)}), s8[4194304]{0:T(1024)(128)(4,1)S(1)}, s32[]{:S(2)}) async-start(s8[4325376]{0:T(1024)(128)(4,1)} %bitcast.82), calls=%async_computation.12 | async-start | bytes 8388608
  135.4 3.6 %copy-start.5 = (bf16[1,1408,8,24]{1,3,2,0:T(8,128)(2,1)S(1)}, bf16[1,1408,8,24]{1,3,2,0:T(8,128)(2,1)}, u32[]{:S(2)}) copy-start(bf16[1,1408,8,24]{1,3,2,0:T(8,128)(2,1)} %copy.59) | copy-start | bytes 1622020
  138.1 2.6 copy-start.3
  140.7 1.6 copy-start.4
  142.3 1.6 copy-start.2
  147.3 8.5 %copy-start.12 = (f32[1536]{0:T(1024)S(1)}, f32[1536]{0:T(1024)}, u32[]{:S(2)}) copy-start(f32[1536]{0:T(1024)} %param.13) | copy-start | bytes 18436
  151.6 11.9 %all-to-all-start = ((bf16[8,96,192]{1,2,0:T(8,128)(2,1)}), bf16[8,96,192]{1,2,0:T(8,128)(2,1)S(1)}, u32[]{:S(2)}, u32[]{:S(2)}) async-start(bf16[8,96,192]{1,2,0:T(8,128)(2,1)} %copy.64), calls=%async_computation | async-start | bytes 786432 | tf_op jit(solution)/shard_map/all_to_all | solution.py:116
  155.8 33.7 %slice-start.1 = ((bf16[8,224256]{1,0:T(8,128)(2,1)}), bf16[8,24576]{1,0:T(8,128)(2,1)S(1)}, s32[]{:S(2)}) async-start(bf16[8,224256]{1,0:T(8,128)(2,1)} %reshape.114), calls=%async_computation.10 | async-start | bytes 786432 | tf_op jit(solution)/shard_map/slice | solution.py:98
  155.8 67.4 %all-gather.16.cloned.1.call-start = ((), (), s32[]{:S(2)}) async-start(), calls=%async_computation.4 | async-start | bytes 1966080 | tf_op jit(solution)/shard_map/all_gather | solution.py:31
  166.9 107.2 %copy-start.8 = (f32[8]{0:T(128)S(1)}, f32[8]{0:T(128)}, u32[]{:S(2)}) copy-start(f32[8]{0:T(128)} %param.16) | copy-start | bytes 100
  189.4 64.4 %all-gather.20.cloned.1.call-start = ((), (), s32[]{:S(2)}) async-start(), calls=%async_computation.6 | async-start | bytes 1966080 | tf_op jit(solution)/shard_map/all_gather | solution.py:31
  190.4 83.6 %all-gather.18.cloned.1.call-start = ((), (), s32[]{:S(2)}) async-start(), calls=%async_computation.5 | async-start | bytes 4718592 | tf_op jit(solution)/shard_map/all_gather | solution.py:32
  223.2 79.9 %all-gather.22.cloned.1.call-start = ((), (), s32[]{:S(2)}) async-start(), calls=%async_computation.7 | async-start | bytes 4718592 | tf_op jit(solution)/shard_map/all_gather | solution.py:32
  283.3 11.1 %copy-start.1 = (bf16[6144,256]{1,0:T(8,128)(2,1)S(1)}, bf16[6144,256]{1,0:T(8,128)(2,1)}, u32[]{:S(2)}) copy-start(bf16[6144,256]{1,0:T(8,128)(2,1)} %all-gather.18.cloned.1.call-done) | copy-start | bytes 9437188
Sparse Core Ops, SparseCore 0:
  13.0 52.6 all-gather.23
  67.6 34.2 all-gather.9
  103.7 31.6 all-gather.11
  137.0 19.5 all-gather.13
  189.6 33.5 all-gather.15
  224.8 28.9 all-gather.19
  255.7 18.3 all-gather.17
  275.8 18.7 all-gather.21
where the time goes:
time: 314 us; the launch traced here: 313 us
  waiting for transfers between devices  147 us (47%)
  local copies, waits for them, and re-layouts  73.3 us (23%)
  matrix products  31.8 us (10%)
  blocking collectives  22.5 us (7%)
  other arithmetic  16.2 us (5%)
  between operations  14.6 us (5%)
  starting transfers between devices  7.52 us (2%)
    all_gather x3, waiting for transfers between devices, spread_in_plane(): inner = lax.all_gather(block, 'sxx', axis=0, tiled=True)  68.2 us
    all_gather x1, waiting for transfers between devices, shards(): got = lax.all_gather(flat, 'sz', axis=0, tiled=False)  51.2 us
    slice x6, local copies, waits for them, and re-layouts, convolve(): kernel[kernel_tap]  26.8 us
    all_gather x1, blocking collectives, shards(): lax.all_gather(keyvals, 'sz', axis=0, tiled=True)  22.5 us
    reshape x1, local copies, waits for them, and re-layouts, shards(): kernel = got[:, :sizes[0]].reshape(nz, taps, ch_in, width).transpose(1, 2...  22.4 us
    all_gather x3, waiting for transfers between devices, spread_in_plane(): return lax.all_gather(inner, 'core', axis=0, tiled=True)  20.2 us
    reduce_sum x1, other arithmetic, attend(): total = jnp.sum(expon, axis=2)  11.1 us
    unnamed x34, local copies, waits for them, and re-layouts  9.51 us
  transfers between devices with their start and end apart: 11, of which 6 were waited for; matrix products, arithmetic and copies ran while one was open for 35% of the time, Pallas kernels for 0%

commit v1 on v0

--- a/solution.py
+++ b/solution.py
@@ -126,7 +126,11 @@
     q_cols = query_weight.shape[1]
     queries = proj[:, :q_cols].astype(jnp.bfloat16)
     keyvals = proj[:, q_cols:].astype(jnp.bfloat16)
-    key_block = spread_in_plane(lax.all_gather(keyvals, "sz", axis=0, tiled=True))
+    key_block = spread_in_plane(
+        jnp.concatenate(
+            lax.all_to_all(jnp.stack([keyvals] * lax.axis_size("sz")), "sz", 0, 0), axis=0
+        )
+    )
     out_weight = spread_in_plane(out_z)
     context = attend(queries, key_block, head_scale)
     projected = jnp.dot(

time: 314 us -> 303 us (0.965)
  waiting for transfers between devices: 147 us -> 138 us
    all_gather x1 -> x0, blocking collectives: 22.5 us -> none  [shards(): lax.all_gather(keyvals, 'sz', axis=0, tiled=True)]
    all_to_all x0 -> x1, blocking collectives: none -> 20 us  [shards(): lax.all_to_all(jnp.stack([keyvals] * lax.axis_size('sz')), 'sz', 0, 0)]
    all_gather x3, waiting for transfers between devices: 68.2 us -> 59.4 us  [spread_in_plane(): inner = lax.all_gather(block, 'sxx', axis=0, tiled=True)]
  transfers between devices with their start and end apart: 11 -> 11, of which waited for: 6 -> 6; matrix products, arithmetic and copies ran while one was open for 35% -> 36% of each run, Pallas kernels for 0% -> 0%
where the time goes in v1:
time: 303 us; the launch traced here: 302 us
  waiting for transfers between devices  138 us (46%)
  local copies, waits for them, and re-layouts  73.3 us (24%)
  matrix products  31.8 us (10%)
  blocking collectives  20 us (7%)
  other arithmetic  16.2 us (5%)
  between operations  14.6 us (5%)
  starting transfers between devices  7.52 us (2%)
    all_gather x3, waiting for transfers between devices, spread_in_plane(): inner = lax.all_gather(block, 'sxx', axis=0, tiled=True)  59.4 us
    all_gather x1, waiting for transfers between devices, shards(): got = lax.all_gather(flat, 'sz', axis=0, tiled=False)  51.2 us
    slice x6, local copies, waits for them, and re-layouts, convolve(): kernel[kernel_tap]  26.8 us
    reshape x1, local copies, waits for them, and re-layouts, shards(): kernel = got[:, :sizes[0]].reshape(nz, taps, ch_in, width).transpose(1, 2...  22.4 us
    all_gather x3, waiting for transfers between devices, spread_in_plane(): return lax.all_gather(inner, 'core', axis=0, tiled=True)  20.2 us
    all_to_all x1, blocking collectives, shards(): lax.all_to_all(jnp.stack([keyvals] * lax.axis_size('sz')), 'sz', 0, 0)  20 us
    reduce_sum x1, other arithmetic, attend(): total = jnp.sum(expon, axis=2)  11.1 us
    unnamed x34, local copies, waits for them, and re-layouts  9.51 us
  transfers between devices with their start and end apart: 11, of which 6 were waited for; matrix products, arithmetic and copies ran while one was open for 36% of the time, Pallas kernels for 0%

profile of v1, /device:TPU:1, one launch (start us, length us, event | category | flops | bytes accessed | tf_op | source)
XLA Modules:
  0.0 301.9 jit_solution(13558590640570256749)
XLA Ops:
  7.3 2.1 copy.56
  9.4 2.4 reshape.105
  12.1 0.8 pad_maximum_fusion.2
  13.1 1.3 fusion.37
  14.5 51.2 %all-gather.24.cloned.1.call-done = bf16[1794048]{0:T(1024)(128)(2,1)} async-done(((bf16[224256]{0:T(1024)(128)(2,1)}), bf16[1794048]{0:T(1024)(128)(2,1)}) %all-gather.24.cloned.1.call-update) | async-done | bytes 3588112 | tf_op jit(solution)/shard_map/all_gather | solution.py:88
  65.7 5.4 %reshape.120 = bf16[8,224256]{1,0:T(8,128)(2,1)} reshape(bf16[1794048]{0:T(1024)(128)(2,1)} %all-gather.24.cloned.1.call-done) | data formatting | bytes 7176192 | tf_op jit(solution)/shard_map/all_gather | solution.py:88
  71.1 1.2 slice.95
  72.3 1.1 reshape.114
  73.6 2.8 reshape.130
  76.4 22.4 %reshape.108 = bf16[8,5,1408,24]{3,2,1,0:T(8,128)(2,1)} reshape(bf16[1351680]{0:T(1024)(128)(2,1)} %reshape.130) | data formatting | bytes 5406720 | tf_op jit(solution)/shard_map/reshape | solution.py:91
  98.8 10.0 %fusion.56 = (bf16[1,1408,8,24]{3,1,0,2:T(8,128)(2,1)S(1)}, bf16[1,1408,8,24]{3,1,0,2:T(8,128)(2,1)}, bf16[1,1408,8,24]{3,1,0,2:T(8,128)(2,1)}, bf16[1,1408,8,24]{3,1,0,2:T(8,128)(2,1)}, bf16[1,1408,8,24]{3,1,0,2:T(8,128)(2,1)}) fusion(bf16[5,1408,8,24]{3,1,0,2:T(8,128)(2,1)} %bitcast.79), kind=kLoop, calls=%fused_computation.61 | loop fusion | bytes 5406720 | tf_op jit(solution)/shard_map/slice | solution.py:20
  108.8 3.7 %copy.58 = bf16[1,1408,8,24]{1,3,2,0:T(8,128)(2,1)} copy(bf16[1,1408,8,24]{3,1,0,2:T(8,128)(2,1)} %get-tuple-element.13) | data formatting | bytes 1081344 | tf_op jit(solution)/shard_map/slice | solution.py:20
  112.5 3.8 %copy.59 = bf16[1,1408,8,24]{1,3,2,0:T(8,128)(2,1)} copy(bf16[1,1408,8,24]{3,1,0,2:T(8,128)(2,1)} %get-tuple-element.12) | data formatting | bytes 1081344 | tf_op jit(solution)/shard_map/slice | solution.py:20
  116.4 3.8 %copy.57 = bf16[1,1408,8,24]{1,3,2,0:T(8,128)(2,1)} copy(bf16[1,1408,8,24]{3,1,0,2:T(8,128)(2,1)} %get-tuple-element.14) | data formatting | bytes 1081344 | tf_op jit(solution)/shard_map/slice | solution.py:20
  120.2 3.8 %copy.61 = bf16[1,1408,8,24]{1,3,2,0:T(8,128)(2,1)} copy(bf16[1,1408,8,24]{3,1,0,2:T(8,128)(2,1)} %get-tuple-element.11) | data formatting | bytes 1081344 | tf_op jit(solution)/shard_map/slice | solution.py:20
  124.0 1.7 copy.60
  125.7 0.8 fusion.57
  126.5 1.3 collective-permute-start
  127.8 1.5 collective-permute-start.1
  129.3 6.1 %all-gather.12.cloned.1.call-done = bf16[768,1280]{1,0:T(8,128)(2,1)} async-done(((bf16[192,1280]{1,0:T(8,128)(2,1)}), bf16[768,1280]{1,0:T(8,128)(2,1)}) %all-gather.12.cloned.1.call-update) | async-done | bytes 1966096 | tf_op jit(solution)/shard_map/all_gather | solution.py:31
  135.4 2.7 constant_dynamic-update-slice_fusion.1
  138.2 0.8 slice-done.3
  139.1 1.6 fusion.58
  140.7 1.6 fusion.12
  142.3 1.6 fusion.8
  143.9 1.6 fusion.26
  145.6 1.7 fusion.20
  147.3 0.3 copy.62
  147.6 0.4 reshape.110
  147.9 2.2 reduce_max.18
  150.3 0.4 convert_element_type.45
  150.8 0.8 copy.64
  151.6 4.2 %all-to-all-start = ((bf16[8,96,192]{1,2,0:T(8,128)(2,1)}), bf16[8,96,192]{1,2,0:T(8,128)(2,1)S(1)}, u32[]{:S(2)}, u32[]{:S(2)}) async-start(bf16[8,96,192]{1,2,0:T(8,128)(2,1)} %copy.64), calls=%async_computation | async-start | bytes 786432 | tf_op jit(solution)/shard_map/all_to_all | solution.py:116
  155.9 7.6 %all-to-all-done = bf16[8,96,192]{1,2,0:T(8,128)(2,1)S(1)} async-done(((bf16[8,96,192]{1,2,0:T(8,128)(2,1)}), bf16[8,96,192]{1,2,0:T(8,128)(2,1)S(1)}, u32[]{:S(2)}, u32[]{:S(2)}) %all-to-all-start) | async-done | bytes 294944 | tf_op jit(solution)/shard_map/all_to_all | solution.py:116
  163.5 0.2 multiply_reduce_fusion
  163.8 0.3 fusion.50
  164.1 2.8 convolution_convert_fusion.1
  166.9 20.0 %all_to_all.10 = bf16[8,96,256]{2,1,0:T(8,128)(2,1)} all-to-all(bf16[8,96,256]{2,1,0:T(8,128)(2,1)S(1)} %stack.2), channel_id=1, replica_groups=mesh['dp'=4,'sz'=8,'sxx'=4,'core'=2] {'sz'}, dimensions={0} | all-to-all | bytes 786432 | tf_op jit(solution)/shard_map/all_to_all | solution.py:131
  187.0 0.9 reshape.118
  188.0 23.8 %all-gather.16.cloned.1.call-done = bf16[3072,256]{1,0:T(8,128)(2,1)} async-done(((bf16[768,256]{1,0:T(8,128)(2,1)}), bf16[3072,256]{1,0:T(8,128)(2,1)}) %all-gather.16.cloned.1.call-update) | async-done | bytes 1572880 | tf_op jit(solution)/shard_map/all_gather | solution.py:31
  211.9 0.3 all-gather.22.cloned.1.call-start
  212.2 0.9 copy.71
  213.1 29.5 %all-gather.20.cloned.1.call-done = bf16[512,1536]{1,0:T(8,128)(2,1)} async-done(((bf16[128,1536]{1,0:T(8,128)(2,1)}), bf16[512,1536]{1,0:T(8,128)(2,1)}) %all-gather.20.cloned.1.call-update) | async-done | bytes 1572880 | tf_op jit(solution)/shard_map/all_gather | solution.py:31
  242.5 20.2 %all-gather.18.cloned.1.call-done = bf16[6144,256]{1,0:T(8,128)(2,1)} async-done(((bf16[3072,256]{1,0:T(8,128)(2,1)}), bf16[6144,256]{1,0:T(8,128)(2,1)}) %all-gather.18.cloned.1.call-update) | async-done | bytes 3145744 | tf_op jit(solution)/shard_map/all_gather | solution.py:32
  262.7 9.2 %bitcast_reduce_fusion = (f32[8,96]{1,0:T(8,128)S(1)}, f32[6144,96,8]{0,1,2:T(8,128)}) fusion(f32[8]{0:T(128)S(1)} %copy-done.8, bf16[6144,256]{1,0:T(8,128)(2,1)} %all-gather.18.cloned.1.call-done, bf16[96,1280]{1,0:T(8,128)(2,1)S(1)} %convolution_convert_fusion.1), kind=kOutput, calls=%fused_computation.1 | convolution fusion | flops 1222114560 | bytes 20647424 | tf_op jit(solution)/shard_map/qhd,kd->hqk/dot_general | solution.py:51
  271.9 11.1 %fusion.1 = f32[8,96]{1,0:T(8,128)S(1)} fusion(f32[6144,96,8]{0,1,2:T(8,128)} %get-tuple-element.18, f32[8,96]{1,0:T(8,128)S(1)} %get-tuple-element.17, f32[8]{0:T(128)S(1)} %copy-done.8), kind=kLoop, calls=%fused_computation.4 | loop fusion | flops 18873600 | bytes 18880544 | tf_op jit(solution)/shard_map/reduce_sum | solution.py:57
  283.1 8.4 %fusion.46 = bf16[96,8,128]{2,0,1:T(8,128)(2,1)S(1)} fusion(bf16[6144,256]{1,0:T(8,128)(2,1)S(1)} %copy-done.1, f32[6144,96,8]{0,1,2:T(8,128)} %get-tuple-element.18, f32[8,96]{1,0:T(8,128)S(1)} %get-tuple-element.17, f32[8]{0:T(128)S(1)} %copy-done.8, f32[96,8]{0,1:T(8,128)S(1)} %bitcast.95), kind=kOutput, calls=%fused_computation.43 | convolution fusion | flops 1227030528 | bytes 20652544 | tf_op jit(solution)/shard_map/hqk,kd->hqd/dot_general | solution.py:58
  291.8 3.3 %convolution_convert_fusion = bf16[96,1536]{1,0:T(8,128)(2,1)} fusion(bf16[96,1024]{0,1:T(8,128)(2,1)S(1)} %bitcast.88, bf16[1024,1536]{1,0:T(8,128)(2,1)} %all-gather.22.cloned.1.call-done), kind=kOutput, calls=%fused_computation.23 | convolution fusion | flops 302137344 | bytes 3637248 | tf_op jit(solution)/shard_map/dot_general | solution.py:136
  (72 shorter events, 1.8 us)
Async XLA Ops:
  7.2 4.6 %copy-start.7 = (bf16[24,1024]{1,0:T(8,128)(2,1)S(1)}, bf16[24,1024]{1,0:T(8,128)(2,1)}, u32[]{:S(2)}) copy-start(bf16[24,1024]{1,0:T(8,128)(2,1)} %param.14) | copy-start | bytes 147460
  7.2 4.6 %copy-start.9 = (bf16[24,256]{1,0:T(8,128)(2,1)S(1)}, bf16[24,256]{1,0:T(8,128)(2,1)}, u32[]{:S(2)}) copy-start(bf16[24,256]{1,0:T(8,128)(2,1)} %param.15) | copy-start | bytes 36868
  7.2 4.8 %copy-start.6 = (bf16[16,1536]{1,0:T(8,128)(2,1)S(1)}, bf16[16,1536]{1,0:T(8,128)(2,1)}, u32[]{:S(2)}) copy-start(bf16[16,1536]{1,0:T(8,128)(2,1)} %param.17) | copy-start | bytes 147460
  7.2 5.7 %copy-start = (bf16[192,1408]{1,0:T(8,128)(2,1)S(1)}, bf16[192,1408]{1,0:T(8,128)(2,1)}, u32[]{:S(2)}) copy-start(bf16[192,1408]{1,0:T(8,128)(2,1)} %param.9) | copy-start | bytes 1622020
  7.2 5.9 %copy-start.10 = (f32[1408]{0:T(1024)S(1)}, f32[1408]{0:T(1024)}, u32[]{:S(2)}) copy-start(f32[1408]{0:T(1024)} %param.10) | copy-start | bytes 16900
  7.2 58.5 %all-gather.24.cloned.1.call-start = ((), (), s32[]{:S(2)}) async-start(), calls=%async_computation.9 | async-start | bytes 4036608 | tf_op jit(solution)/shard_map/all_gather | solution.py:88
  12.9 112.8 %all-gather.10.cloned.1.call-start = ((), (), s32[]{:S(2)}) async-start(), calls=%async_computation.2 | async-start | bytes 4866048 | tf_op jit(solution)/shard_map/all_gather | solution.py:102
  14.5 59.0 %copy-start.11 = (f32[1536]{0:T(1024)S(1)}, f32[1536]{0:T(1024)}, u32[]{:S(2)}) copy-start(f32[1536]{0:T(1024)} %param.12) | copy-start | bytes 18436
  14.5 120.9 %all-gather.12.cloned.1.call-start = ((), (), s32[]{:S(2)}) async-start(), calls=%async_computation.3 | async-start | bytes 2457600 | tf_op jit(solution)/shard_map/all_gather | solution.py:31
  71.1 2.6 slice-start
  73.4 90.7 %all-gather.14.cloned.1.call-start = ((), (), s32[]{:S(2)}) async-start(), calls=%async_computation.4 | async-start | bytes 5898240 | tf_op jit(solution)/shard_map/all_gather | solution.py:32
  126.5 14.2 %collective-permute-start = (bf16[2,1408]{1,0:T(2,128)(2,1)S(1)}, bf16[2,1408]{1,0:T(2,128)(2,1)S(1)}, u32[]{:S(2)}, u32[]{:S(2)}) collective-permute-start(bf16[2,1408]{1,0:T(2,128)(2,1)S(1)} %get-tuple-element.15), channel_id=1, source_target_pairs={{0,8},{8,16},{16,24},{24,32},{32,40},{40,48},{48,56},{1,9},{9,17},... | collective-permute-start | bytes 16904 | tf_op jit(solution)/shard_map/ppermute | solution.py:106
  127.8 12.8 %collective-permute-start.1 = (bf16[2,1408]{1,0:T(2,128)(2,1)S(1)}, bf16[2,1408]{1,0:T(2,128)(2,1)S(1)}, u32[]{:S(2)}, u32[]{:S(2)}) collective-permute-start(bf16[2,1408]{1,0:T(2,128)(2,1)S(1)} %get-tuple-element.16), channel_id=1, source_target_pairs={{8,0},{16,8},{24,16},{32,24},{40,32},{48,40},{56,48},{9,1},{17,9},... | collective-permute-start | bytes 16904 | tf_op jit(solution)/shard_map/ppermute | solution.py:107
  135.4 2.8 slice-start.2
  135.4 3.5 %slice-start.3 = ((s8[4325376]{0:T(1024)(128)(4,1)}), s8[4194304]{0:T(1024)(128)(4,1)S(1)}, s32[]{:S(2)}) async-start(s8[4325376]{0:T(1024)(128)(4,1)} %bitcast.83), calls=%async_computation.13 | async-start | bytes 8388608
  135.4 3.6 %copy-start.5 = (bf16[1,1408,8,24]{1,3,2,0:T(8,128)(2,1)S(1)}, bf16[1,1408,8,24]{1,3,2,0:T(8,128)(2,1)}, u32[]{:S(2)}) copy-start(bf16[1,1408,8,24]{1,3,2,0:T(8,128)(2,1)} %copy.59) | copy-start | bytes 1622020
  138.1 2.6 copy-start.3
  140.7 1.6 copy-start.4
  142.3 1.6 copy-start.2
  147.3 8.5 %copy-start.12 = (f32[1536]{0:T(1024)S(1)}, f32[1536]{0:T(1024)}, u32[]{:S(2)}) copy-start(f32[1536]{0:T(1024)} %param.13) | copy-start | bytes 18436
  151.6 11.9 %all-to-all-start = ((bf16[8,96,192]{1,2,0:T(8,128)(2,1)}), bf16[8,96,192]{1,2,0:T(8,128)(2,1)S(1)}, u32[]{:S(2)}, u32[]{:S(2)}) async-start(bf16[8,96,192]{1,2,0:T(8,128)(2,1)} %copy.64), calls=%async_computation | async-start | bytes 786432 | tf_op jit(solution)/shard_map/all_to_all | solution.py:116
  155.8 56.0 %all-gather.16.cloned.1.call-start = ((), (), s32[]{:S(2)}) async-start(), calls=%async_computation.5 | async-start | bytes 1966080 | tf_op jit(solution)/shard_map/all_gather | solution.py:31
  163.7 23.2 %slice-start.1 = ((bf16[8,224256]{1,0:T(8,128)(2,1)}), bf16[8,24576]{1,0:T(8,128)(2,1)S(1)}, s32[]{:S(2)}) async-start(bf16[8,224256]{1,0:T(8,128)(2,1)} %reshape.120), calls=%async_computation.11 | async-start | bytes 786432 | tf_op jit(solution)/shard_map/slice | solution.py:98
  166.9 95.8 %copy-start.8 = (f32[8]{0:T(128)S(1)}, f32[8]{0:T(128)}, u32[]{:S(2)}) copy-start(f32[8]{0:T(128)} %param.16) | copy-start | bytes 100
  186.9 55.6 %all-gather.20.cloned.1.call-start = ((), (), s32[]{:S(2)}) async-start(), calls=%async_computation.7 | async-start | bytes 1966080 | tf_op jit(solution)/shard_map/all_gather | solution.py:31
  188.0 74.8 %all-gather.18.cloned.1.call-start = ((), (), s32[]{:S(2)}) async-start(), calls=%async_computation.6 | async-start | bytes 4718592 | tf_op jit(solution)/shard_map/all_gather | solution.py:32
  211.9 79.9 %all-gather.22.cloned.1.call-start = ((), (), s32[]{:S(2)}) async-start(), calls=%async_computation.8 | async-start | bytes 4718592 | tf_op jit(solution)/shard_map/all_gather | solution.py:32
  271.9 11.1 %copy-start.1 = (bf16[6144,256]{1,0:T(8,128)(2,1)S(1)}, bf16[6144,256]{1,0:T(8,128)(2,1)}, u32[]{:S(2)}) copy-start(bf16[6144,256]{1,0:T(8,128)(2,1)} %all-gather.18.cloned.1.call-done) | copy-start | bytes 9437188
Sparse Core Ops, SparseCore 0:
  13.0 52.6 all-gather.23
  67.6 34.2 all-gather.9
  103.7 31.6 all-gather.11
  137.0 19.5 all-gather.13
  187.1 24.7 all-gather.15
  213.5 28.9 all-gather.19
  244.3 18.3 all-gather.17
  264.5 18.7 all-gather.21
